TPU v7x, 32 devices: a whole 2x2x4 slice. The times are simulated.
32 devices in a mesh: group: 16 (over z, x, core), slab: 2 (over y).
Axes of the slice: x: 2, y: 2, z: 4, core: 2. Of those that a mesh axis runs over, the one named last changes fastest.
Arguments:
- tokens: bfloat16 [16, 1024, 1024], P('group', 'slab'), may hold values from -6 to 6
- norm_gain: float32 [1024], replicated, may hold values from 0.1 to 1.9
- w_qkv: bfloat16 [1024, 3, 1024], P(None, None, 'slab'), may hold values from -0.1875 to 0.1875
- q_gain: float32 [64], replicated, may hold values from 0.5 to 3
- k_gain: float32 [64], replicated, may hold values from 0.5 to 3
- w_out: bfloat16 [1024, 1024], P('slab'), may hold values from -0.1875 to 0.1875
- covis_mask: int32 [16, 16], replicated, may hold values from 0 to 1, as said below
- capture_rank: int32 [16], replicated, may hold values from 0 to 15, each once
Outputs:
- mixed_rows: bfloat16 [16, 1024, 1024], P('group', 'slab')
Inputs may be any that keep to these rules, and one draw needn't show every extreme that they name: covis_mask[i, j] is 1 where i = j, 0 where |i - j| > 3, and covis_mask[i, j] = covis_mask[j, i]. `capture_rank`: a permutation of the image numbers.
All inputs are finite; a program needn't handle non-finite values.
Results may differ from a plain program's by a relative error of at most 0.015.
The roundings to bfloat16 on the way count: a program that leaves them out, or rounds other values in their place, can miss the bound.
Values may be sent and summed in bfloat16 or wider, within the bound.
No kernel may reach another device: no remote copies, remote signals or barrier semaphores. Data moves between devices by JAX's collectives and lax.ppermute only.
A program may use at most 64 MiB of HBM per device.

v0:
```python
import jax
import jax.numpy as jnp
from jax import lax
from jax.sharding import PartitionSpec as P

REACH = 3


def shifted(block, axis, distance):
    devices = range(lax.axis_size(axis))
    route = [(i - distance, i) for i in devices if i - distance in devices]
    return lax.ppermute(block, axis, route)


def rotated(block, axis, distance):
    count = lax.axis_size(axis)
    route = [(i, (i + distance) % count) for i in range(count)]
    return lax.ppermute(block, axis, route)


def norm_rows(values, gain):
    centre = jnp.mean(values, axis=-1, keepdims=True)
    centred = values - centre
    spread = jnp.mean(centred * centred, axis=-1, keepdims=True)
    return centred * lax.rsqrt(spread + 1e-06) * gain


def block_terms(queries, key_rows, values, score_scale):
    scores = (
        jnp.einsum("qhd,khd->hqk", queries, key_rows, preferred_element_type=jnp.float32)
        * score_scale
    )
    weights = jnp.exp(scores).astype(jnp.bfloat16)
    numerator = jnp.einsum("hqk,khd->qhd", weights, values, preferred_element_type=jnp.float32)
    denominator = jnp.transpose(jnp.sum(weights, axis=2, dtype=jnp.float32))
    return (numerator, denominator)


def set_terms(queries, key_sets, score_scale):
    numerator, denominator = None, None
    for key_rows, values in key_sets:
        part_num, part_den = block_terms(queries, key_rows, values, score_scale)
        if numerator is None:
            numerator, denominator = part_num, part_den
        else:
            numerator, denominator = numerator + part_num, denominator + part_den
    return numerator, denominator


def body(tokens, norm_gain, w_qkv, q_gain, k_gain, w_out, covis_mask, capture_rank):
    full_width = tokens.shape[2]
    local_width = w_qkv.shape[2]
    head_size = q_gain.shape[0]
    heads_here = local_width // head_size
    score_scale = head_size ** (-0.5)
    slab_count = lax.axis_size("slab")
    my_group = lax.axis_index("group")
    group_count = lax.axis_size("group")
    normed = norm_rows(tokens[0].astype(jnp.float32), norm_gain).astype(jnp.bfloat16)
    piece_rows = normed.shape[0]
    flat_w = w_qkv.reshape(full_width, 3 * local_width)

    def project(rows):
        projected = jnp.dot(rows, flat_w, preferred_element_type=jnp.float32)
        projected = projected.reshape(rows.shape[0], 3, heads_here, head_size)
        queries = norm_rows(projected[:, 0], q_gain).astype(jnp.bfloat16)
        key_rows = norm_rows(projected[:, 1], k_gain).astype(jnp.bfloat16)
        values = projected[:, 2].astype(jnp.bfloat16)
        return queries, jnp.stack([key_rows, values], axis=1)

    queries, pairs = project(normed)
    if slab_count > 1:
        others = jnp.concatenate(
            [rotated(normed, "slab", k) for k in range(1, slab_count)], axis=0
        )
        rest_q, rest_pairs = project(others)
        queries = jnp.concatenate([queries, rest_q], axis=0)
        pairs = jnp.concatenate([pairs, rest_pairs], axis=0)
    token_count = queries.shape[0]

    def allowed_from(source):
        in_range = (source >= 0) & (source < group_count)
        clipped = jnp.clip(source, 0, group_count - 1)
        return (
            in_range
            & (covis_mask[my_group, clipped] == 1)
            & (capture_rank[clipped] <= capture_rank[my_group])
        )

    def pair_terms(rows, held):
        return block_terms(queries[rows], held[:, 0], held[:, 1], score_scale)

    def masked_terms(source, rows, held):
        row_count = rows.stop - rows.start

        def skipped():
            return (
                jnp.zeros((row_count, heads_here, head_size), jnp.float32),
                jnp.zeros((row_count, heads_here), jnp.float32),
            )

        return lax.cond(allowed_from(source), lambda: pair_terms(rows, held), skipped)

    def routed(block, route):
        return lax.ppermute(block, "group", [(a, b) for a, b in route if 0 <= b < group_count])

    g_all = range(group_count)
    spot = my_group % 4
    low = spot < 2
    even = spot % 2 == 0
    on_chip = [(g, g ^ 1) for g in g_all]
    across_x = [(g, g ^ 2) for g in g_all]
    along_z_once = [(g, g + 3) if g % 2 == 1 else (g, g - 3) for g in g_all]
    along_z_relay = [(g, g + 4) if g % 4 < 2 else (g, g - 4) for g in g_all]

    all_rows = slice(0, token_count)
    round_one = [
        (my_group ^ 1, routed(pairs, on_chip)),
        (my_group ^ 2, routed(pairs, across_x)),
        (jnp.where(even, my_group - 3, my_group + 3), routed(pairs, along_z_once)),
    ]
    numerator, denominator = pair_terms(all_rows, pairs)
    round_one, numerator, denominator = lax.optimization_barrier((round_one, numerator, denominator))
    from_x = round_one[1][1]
    round_two = [
        (my_group ^ 3, routed(from_x, on_chip)),
        (jnp.where(low, my_group - 2, my_group + 2), routed(from_x, along_z_relay)),
    ]
    for source, held in round_one:
        part_num, part_den = masked_terms(source, all_rows, held)
        numerator, denominator = numerator + part_num, denominator + part_den
    round_two, numerator, denominator = lax.optimization_barrier((round_two, numerator, denominator))
    from_z = round_two[1][1]
    last_source = jnp.where(
        spot == 0, my_group - 1, jnp.where(spot == 1, my_group - 3, jnp.where(spot == 2, my_group + 3, my_group + 1))
    )
    last_held = routed(from_z, on_chip)
    for source, held in round_two:
        part_num, part_den = masked_terms(source, all_rows, held)
        numerator, denominator = numerator + part_num, denominator + part_den
    last_held, numerator, denominator = lax.optimization_barrier((last_held, numerator, denominator))

    mixed = None
    for k in list(range(1, slab_count)) + [0]:
        rows = slice(k * piece_rows, (k + 1) * piece_rows)
        part_num, part_den = masked_terms(last_source, rows, last_held)
        chunk_num, chunk_den = numerator[rows] + part_num, denominator[rows] + part_den
        attended = (
            (chunk_num / chunk_den[:, :, None]).astype(jnp.bfloat16).reshape(piece_rows, local_width)
        )
        chunk = jnp.dot(attended, w_out, preferred_element_type=jnp.float32)
        if k != 0:
            outgoing, last_held, numerator, denominator = lax.optimization_barrier(
                (chunk.astype(jnp.bfloat16), last_held, numerator, denominator)
            )
            chunk = rotated(outgoing, "slab", -k).astype(jnp.float32)
        mixed = chunk if mixed is None else mixed + chunk
    return mixed.astype(jnp.bfloat16)[None]


def solution(mesh):
    placed = (
        P("group", "slab", None),
        P(),
        P(None, None, "slab"),
        P(),
        P(),
        P("slab", None),
        P(),
        P(),
    )
    return jax.shard_map(
        body, mesh=mesh, in_specs=placed, out_specs=P("group", "slab", None), check_vma=False
    )
```

profile of v0, /device:TPU:20, one launch (start us, length us, event | category | flops | bytes accessed | tf_op | source)
XLA Modules:
  0.0 246.7 jit_solution(11463756480646542694)
XLA Ops:
  0.0 1.6 convert_reduce_fusion.8
  1.6 1.6 fusion.34
  3.3 0.4 fusion.36
  3.7 0.6 collective-permute-start
  4.2 4.6 %copy.20 = bf16[1024,3,512]{0,2,1:T(8,128)(2,1)} copy(bf16[1024,3,512]{2,0,1:T(8,128)(2,1)} %param.24) | data formatting | bytes 6291456 | tf_op args[2]
  8.9 5.5 %fusion.39 = f32[512,3,8,64]{0,3,2,1:T(8,128)} fusion(bf16[3,8,64,1024]{3,2,1,0:T(8,128)(2,1)} %bitcast.180, bf16[1,512,1024]{2,1,0:T(8,128)(2,1)S(1)} %copy-done.2, f32[1024]{0:T(1024)S(1)} %copy-done.18, f32[512]{0:T(512)S(1)} %add_rsqrt_fusion.4, f32[512]{0:T(512)S(1)} %broadcast_multiply_fusion.4), kind=kOutput, calls=%fused_computation.71 | convolution fusion | flops 1613234176 | bytes 7348224 | tf_op jit(solution)/shard_map/dot_general | solution.py:64
  14.4 1.3 slice.179
  15.7 2.0 slice_reduce_fusion.1
  17.7 1.9 multiply_reduce_fusion.1
  19.6 9.1 %collective-permute-done = bf16[512,1024]{1,0:T(8,128)(2,1)} collective-permute-done((bf16[512,1024]{1,0:T(8,128)(2,1)S(1)}, bf16[512,1024]{1,0:T(8,128)(2,1)}, u32[]{:S(2)}, u32[]{:S(2)}) %collective-permute-start) | collective-permute-done | bytes 1048608 | tf_op jit(solution)/shard_map/ppermute | solution.py:18
  28.7 3.1 %fusion.41 = f32[512,3,8,64]{0,3,2,1:T(8,128)S(1)} fusion(bf16[3,8,64,1024]{3,2,1,0:T(8,128)(2,1)S(1)} %bitcast.181, bf16[512,1024]{1,0:T(8,128)(2,1)} %collective-permute-done), kind=kOutput, calls=%fused_computation.77 | convolution fusion | flops 1610612736 | bytes 7340032 | tf_op jit(solution)/shard_map/dot_general | solution.py:64
  31.8 0.3 slice_reduce_fusion
  32.1 0.0 copy-start.19
  32.1 0.1 slice.178
  32.2 0.3 multiply_reduce_fusion
  32.6 1.4 copy-done.1
  34.0 0.5 multiply_convert_fusion.3
  34.5 0.3 maximum_maximum_fusion
  34.8 0.1 collective-permute-start.1
  34.9 1.6 collective-permute-start.2
  36.4 2.6 %collective-permute-start.3 = (bf16[1024,2,8,64]{0,3,2,1:T(8,128)(2,1)S(1)}, bf16[1024,2,8,64]{0,3,2,1:T(8,128)(2,1)S(1)}, u32[]{:S(2)}, u32[]{:S(2)}) collective-permute-start(bf16[1024,2,8,64]{0,3,2,1:T(8,128)(2,1)S(1)} %maximum_maximum_fusion), channel_id=1, source_target_pairs={{2,8},{6,12},{8,2},{10,16},{12,6},{14,20},{16,10},{18,24},{20,14},... | collective-permute-start | bytes 6291464 | tf_op jit(solution)/shard_map/ppermute | solution.py:105
  39.0 0.5 multiply_convert_fusion.1
  39.6 9.0 %convert_reduce_fusion.7 = (f32[8,1024]{1,0:T(8,128)S(1)}, bf16[8,1024,1024]{1,2,0:T(8,128)(2,1)}) fusion(bf16[1024,2,8,64]{0,3,2,1:T(8,128)(2,1)S(1)} %maximum_maximum_fusion, bf16[512,8,64]{0,2,1:T(8,128)(2,1)S(1)} %get-tuple-element.153, bf16[512,8,64]{0,2,1:T(8,128)(2,1)S(1)} %get-tuple-element.152), kind=kOutput, calls=%fused_computation.49 | convolution fusion | flops 1109385216 | bytes 18907136 | tf_op jit(solution)/shard_map/qhd,khd->hqk/dot_general | solution.py:30
  48.6 8.8 %convolution_bitcast_fusion.7 = f32[1024,8,64]{0,2,1:T(8,128)S(1)} fusion(bf16[8,1024,1024]{1,2,0:T(8,128)(2,1)} %get-tuple-element.157, bf16[1024,2,8,64]{0,3,2,1:T(8,128)(2,1)S(1)} %maximum_maximum_fusion), kind=kOutput, calls=%fused_computation.67 | convolution fusion | flops 1073741824 | bytes 19922944 | tf_op jit(solution)/shard_map/hqk,khd->qhd/dot_general | solution.py:34
  57.5 25.5 %collective-permute-done.2 = bf16[1024,2,8,64]{0,3,2,1:T(8,128)(2,1)} collective-permute-done((bf16[1024,2,8,64]{0,3,2,1:T(8,128)(2,1)S(1)}, bf16[1024,2,8,64]{0,3,2,1:T(8,128)(2,1)}, u32[]{:S(2)}, u32[]{:S(2)}) %collective-permute-start.2) | collective-permute-done | bytes 2097184 | tf_op jit(solution)/shard_map/ppermute | solution.py:105
  83.0 1.3 copy-done.13
  84.4 3.5 %collective-permute-start.5 = (bf16[1024,2,8,64]{0,3,2,1:T(8,128)(2,1)}, bf16[1024,2,8,64]{0,3,2,1:T(8,128)(2,1)}, u32[]{:S(2)}, u32[]{:S(2)}) collective-permute-start(bf16[1024,2,8,64]{0,3,2,1:T(8,128)(2,1)} %collective-permute-done.2), channel_id=1, source_target_pairs={{0,8},{2,10},{8,16},{10,18},{12,4},{14,6},{16,24},{18,26},{20,12},... | collective-permute-start | bytes 6291464 | tf_op jit(solution)/shard_map/ppermute | solution.py:105
  87.9 2.3 pad_maximum_fusion
  90.2 0.6 fusion.53
  92.0 1.4 fusion.51
  97.6 19.7 %conditional.7 = (f32[1024,8,64]{0,2,1:T(8,128)S(1)}, f32[1024,8]{0,1:T(8,128)S(1)}) conditional(s32[]{:T(128)} %convert_element_type.126, () %tuple.66, (bf16[1024,2,8,64]{0,3,2,1:T(8,128)(2,1)}, bf16[1024,8,64]{0,2,1:T(8,128)(2,1)}) %tuple.125), branch_computations={%region_11.12_spmd, %region_12.14_spmd} | conditional | flops 2181029888 | bytes 47218732 | solution.py:102
  97.7 10.9 %convert_reduce_fusion = (f32[8,1024]{1,0:T(8,128)S(1)}, bf16[8,1024,1024]{1,2,0:T(8,128)(2,1)}) fusion(bf16[1024,8,64]{0,2,1:T(8,128)(2,1)} %get-tuple-element.33, bf16[1024,2,8,64]{0,3,2,1:T(8,128)(2,1)} %get-tuple-element.34), kind=kOutput, calls=%fused_computation | convolution fusion | flops 1107288064 | bytes 18907136 | tf_op jit(solution)/shard_map/cond/branch_1_fun/qhd,khd->hqk/dot_general | solution.py:30
  108.5 8.8 %convolution_bitcast_fusion = f32[1024,8,64]{0,2,1:T(8,128)S(1)} fusion(bf16[8,1024,1024]{1,2,0:T(8,128)(2,1)} %get-tuple-element.126, bf16[1024,2,8,64]{0,3,2,1:T(8,128)(2,1)S(1)} %copy-done.16), kind=kOutput, calls=%fused_computation.2 | convolution fusion | flops 1073741824 | bytes 19922944 | tf_op jit(solution)/shard_map/cond/branch_1_fun/hqk,khd->qhd/dot_general | solution.py:34
  117.3 1.4 copy-done.3
  118.7 20.0 %conditional.8 = (f32[1024,8,64]{0,2,1:T(8,128)S(1)}, f32[1024,8]{0,1:T(8,128)S(1)}) conditional(s32[]{:T(128)} %convert_element_type.127, () %tuple.68, (bf16[1024,2,8,64]{0,3,2,1:T(8,128)(2,1)}, bf16[1024,8,64]{0,2,1:T(8,128)(2,1)}) %tuple.69), branch_computations={%region_14.15_spmd, %region_15.17_spmd} | conditional | flops 2181029888 | bytes 38830096 | solution.py:102
  118.9 10.7 %convert_reduce_fusion.1 = (f32[8,1024]{1,0:T(8,128)S(1)}, bf16[8,1024,1024]{1,2,0:T(8,128)(2,1)}) fusion(bf16[1024,8,64]{0,2,1:T(8,128)(2,1)} %get-tuple-element.35, bf16[1024,2,8,64]{0,3,2,1:T(8,128)(2,1)} %get-tuple-element.36), kind=kOutput, calls=%fused_computation.7 | convolution fusion | flops 1107288064 | bytes 18907136 | tf_op jit(solution)/shard_map/cond/branch_1_fun/qhd,khd->hqk/dot_general | solution.py:30
  129.6 9.1 %convolution_bitcast_fusion.1 = f32[1024,8,64]{0,2,1:T(8,128)S(1)} fusion(bf16[8,1024,1024]{1,2,0:T(8,128)(2,1)} %get-tuple-element.128, bf16[1024,2,8,64]{0,3,2,1:T(8,128)(2,1)} %get-tuple-element.36), kind=kOutput, calls=%fused_computation.9 | convolution fusion | flops 1073741824 | bytes 19922944 | tf_op jit(solution)/shard_map/cond/branch_1_fun/hqk,khd->qhd/dot_general | solution.py:34
  138.7 1.3 copy-done.4
  140.0 19.7 %conditional.9 = (f32[1024,8,64]{0,2,1:T(8,128)S(1)}, f32[1024,8]{0,1:T(8,128)S(1)}) conditional(s32[]{:T(128)} %convert_element_type.128, () %tuple.70, (bf16[1024,2,8,64]{0,3,2,1:T(8,128)(2,1)}, bf16[1024,8,64]{0,2,1:T(8,128)(2,1)}) %tuple.124), branch_computations={%region_17.18_spmd, %region_18.20_spmd} | conditional | flops 2181029888 | bytes 47218732 | solution.py:102
  140.0 10.8 %convert_reduce_fusion.2 = (f32[8,1024]{1,0:T(8,128)S(1)}, bf16[8,1024,1024]{1,2,0:T(8,128)(2,1)}) fusion(bf16[1024,8,64]{0,2,1:T(8,128)(2,1)} %get-tuple-element.37, bf16[1024,2,8,64]{0,3,2,1:T(8,128)(2,1)} %get-tuple-element.38), kind=kOutput, calls=%fused_computation.14 | convolution fusion | flops 1107288064 | bytes 18907136 | tf_op jit(solution)/shard_map/cond/branch_1_fun/qhd,khd->hqk/dot_general | solution.py:30
  150.9 8.8 %convolution_bitcast_fusion.2 = f32[1024,8,64]{0,2,1:T(8,128)S(1)} fusion(bf16[8,1024,1024]{1,2,0:T(8,128)(2,1)} %get-tuple-element.130, bf16[1024,2,8,64]{0,3,2,1:T(8,128)(2,1)S(1)} %copy-done.14), kind=kOutput, calls=%fused_computation.16 | convolution fusion | flops 1073741824 | bytes 19922944 | tf_op jit(solution)/shard_map/cond/branch_1_fun/hqk,khd->qhd/dot_general | solution.py:34
  159.7 4.5 %add_add_fusion.1 = f32[1024,8,64]{0,2,1:T(8,128)} fusion(f32[1024,8,64]{0,2,1:T(8,128)S(1)} %get-tuple-element.91, f32[1024,8,64]{0,2,1:T(8,128)} %copy-done.4, f32[1024,8,64]{0,2,1:T(8,128)S(1)} %convolution_bitcast_fusion.7, f32[1024,8,64]{0,2,1:T(8,128)} %copy-done.3), kind=kLoop, calls=%fused_computation.66 | loop fusion | flops 1572864 | bytes 10485760 | tf_op jit(solution)/shard_map/add | solution.py:131
  164.3 0.7 fusion.52
  166.3 1.5 fusion.50
  172.1 20.1 %conditional.10 = (f32[1024,8,64]{0,2,1:T(8,128)S(1)}, f32[1024,8]{0,1:T(8,128)S(1)}) conditional(s32[]{:T(128)} %convert_element_type.129, () %tuple.73, (bf16[1024,2,8,64]{0,3,2,1:T(8,128)(2,1)}, bf16[1024,8,64]{0,2,1:T(8,128)(2,1)}) %tuple.74), branch_computations={%region_20.21_spmd, %region_21.23_spmd} | conditional | flops 2181029888 | bytes 38830096 | solution.py:102
  172.3 10.7 %convert_reduce_fusion.3 = (f32[8,1024]{1,0:T(8,128)S(1)}, bf16[8,1024,1024]{1,2,0:T(8,128)(2,1)}) fusion(bf16[1024,8,64]{0,2,1:T(8,128)(2,1)} %get-tuple-element.39, bf16[1024,2,8,64]{0,3,2,1:T(8,128)(2,1)} %get-tuple-element.40), kind=kOutput, calls=%fused_computation.21 | convolution fusion | flops 1107288064 | bytes 18907136 | tf_op jit(solution)/shard_map/cond/branch_1_fun/qhd,khd->hqk/dot_general | solution.py:30
  183.0 9.1 %convolution_bitcast_fusion.3 = f32[1024,8,64]{0,2,1:T(8,128)S(1)} fusion(bf16[8,1024,1024]{1,2,0:T(8,128)(2,1)} %get-tuple-element.132, bf16[1024,2,8,64]{0,3,2,1:T(8,128)(2,1)} %get-tuple-element.40), kind=kOutput, calls=%fused_computation.23 | convolution fusion | flops 1073741824 | bytes 19922944 | tf_op jit(solution)/shard_map/cond/branch_1_fun/hqk,khd->qhd/dot_general | solution.py:34
  192.2 1.3 copy-done.7
  193.5 19.9 %conditional.11 = (f32[1024,8,64]{0,2,1:T(8,128)S(1)}, f32[1024,8]{0,1:T(8,128)S(1)}) conditional(s32[]{:T(128)} %convert_element_type.130, () %tuple.75, (bf16[1024,2,8,64]{0,3,2,1:T(8,128)(2,1)}, bf16[1024,8,64]{0,2,1:T(8,128)(2,1)}) %tuple.76), branch_computations={%region_23.24_spmd, %region_24.26_spmd} | conditional | flops 2181029888 | bytes 38830096 | solution.py:102
  193.5 10.8 %convert_reduce_fusion.4 = (f32[8,1024]{1,0:T(8,128)S(1)}, bf16[8,1024,1024]{1,2,0:T(8,128)(2,1)}) fusion(bf16[1024,8,64]{0,2,1:T(8,128)(2,1)} %get-tuple-element.41, bf16[1024,2,8,64]{0,3,2,1:T(8,128)(2,1)} %get-tuple-element.42), kind=kOutput, calls=%fused_computation.28 | convolution fusion | flops 1107288064 | bytes 18907136 | tf_op jit(solution)/shard_map/cond/branch_1_fun/qhd,khd->hqk/dot_general | solution.py:30
  204.2 9.1 %convolution_bitcast_fusion.4 = f32[1024,8,64]{0,2,1:T(8,128)S(1)} fusion(bf16[8,1024,1024]{1,2,0:T(8,128)(2,1)} %get-tuple-element.134, bf16[1024,2,8,64]{0,3,2,1:T(8,128)(2,1)} %get-tuple-element.42), kind=kOutput, calls=%fused_computation.30 | convolution fusion | flops 1073741824 | bytes 19922944 | tf_op jit(solution)/shard_map/cond/branch_1_fun/hqk,khd->qhd/dot_general | solution.py:34
  213.4 3.7 %add_add_fusion = f32[1024,8,64]{0,2,1:T(8,128)} fusion(f32[1024,8,64]{0,2,1:T(8,128)S(1)} %get-tuple-element.102, f32[1024,8,64]{0,2,1:T(8,128)S(1)} %copy-done.5, f32[1024,8,64]{0,2,1:T(8,128)} %copy-done.7), kind=kLoop, calls=%fused_computation.65 | loop fusion | flops 1048576 | bytes 8388608 | tf_op jit(solution)/shard_map/add | solution.py:140
  217.1 9.1 %conditional.12 = (f32[512,8,64]{0,2,1:T(8,128)S(1)}, f32[512,8]{0,1:T(8,128)S(1)}) conditional(s32[]{:T(128)} %convert_element_type.131, () %tuple.78, (bf16[1024,2,8,64]{0,3,2,1:T(8,128)(2,1)}, bf16[512,8,64]{0,2,1:T(8,128)(2,1)S(1)}) %tuple.123), branch_computations={%region_26.27_spmd, %region_27.29_spmd} | conditional | flops 1090514944 | bytes 20463632 | solution.py:102
  217.4 4.9 %convert_reduce_fusion.5 = (f32[8,512]{1,0:T(8,128)S(1)}, bf16[8,512,1024]{2,1,0:T(8,128)(2,1)S(1)}) fusion(bf16[512,8,64]{0,2,1:T(8,128)(2,1)S(1)} %get-tuple-element.43, bf16[1024,2,8,64]{0,3,2,1:T(8,128)(2,1)} %get-tuple-element.44), kind=kOutput, calls=%fused_computation.35 | convolution fusion | flops 553644032 | bytes 9977856 | tf_op jit(solution)/shard_map/cond/branch_1_fun/qhd,khd->hqk/dot_general | solution.py:30
  222.3 3.9 %convolution_bitcast_fusion.5 = f32[512,8,64]{0,2,1:T(8,128)S(1)} fusion(bf16[8,512,1024]{2,1,0:T(8,128)(2,1)S(1)} %get-tuple-element.136, bf16[1024,2,8,64]{0,3,2,1:T(8,128)(2,1)} %get-tuple-element.44), kind=kOutput, calls=%fused_computation.37 | convolution fusion | flops 536870912 | bytes 10485760 | tf_op jit(solution)/shard_map/cond/branch_1_fun/hqk,khd->qhd/dot_general | solution.py:34
  226.2 0.3 divide_convert_fusion.1
  226.5 1.7 convolution_convert_fusion
  228.2 0.5 collective-permute-start.7
  228.7 8.6 %conditional.13 = (f32[512,8,64]{0,2,1:T(8,128)S(1)}, f32[512,8]{0,1:T(8,128)S(1)}) conditional(s32[]{:T(128)} %convert_element_type.131, () %tuple.81, (bf16[1024,2,8,64]{0,3,2,1:T(8,128)(2,1)}, bf16[512,8,64]{0,2,1:T(8,128)(2,1)S(1)}) %tuple.122), branch_computations={%region_29.30_spmd, %region_30.32_spmd} | conditional | flops 1090514944 | bytes 20463632 | solution.py:102
  228.7 4.7 %convert_reduce_fusion.6 = (f32[8,512]{1,0:T(8,128)S(1)}, bf16[8,512,1024]{2,1,0:T(8,128)(2,1)S(1)}) fusion(bf16[512,8,64]{0,2,1:T(8,128)(2,1)S(1)} %get-tuple-element.45, bf16[1024,2,8,64]{0,3,2,1:T(8,128)(2,1)} %get-tuple-element.46), kind=kOutput, calls=%fused_computation.42 | convolution fusion | flops 553644032 | bytes 9977856 | tf_op jit(solution)/shard_map/cond/branch_1_fun/qhd,khd->hqk/dot_general | solution.py:30
  233.4 3.9 %convolution_bitcast_fusion.6 = f32[512,8,64]{0,2,1:T(8,128)S(1)} fusion(bf16[8,512,1024]{2,1,0:T(8,128)(2,1)S(1)} %get-tuple-element.138, bf16[1024,2,8,64]{0,3,2,1:T(8,128)(2,1)} %get-tuple-element.46), kind=kOutput, calls=%fused_computation.44 | convolution fusion | flops 536870912 | bytes 10485760 | tf_op jit(solution)/shard_map/cond/branch_1_fun/hqk,khd->qhd/dot_general | solution.py:34
  237.3 0.3 divide_convert_fusion
  237.6 5.7 %collective-permute-done.7 = bf16[512,1024]{1,0:T(8,128)(2,1)} collective-permute-done((bf16[512,1024]{1,0:T(8,128)(2,1)}, bf16[512,1024]{1,0:T(8,128)(2,1)}, u32[]{:S(2)}, u32[]{:S(2)}) %collective-permute-start.7) | collective-permute-done | bytes 1048608 | tf_op jit(solution)/shard_map/ppermute | solution.py:18
  243.3 2.9 %fusion.37 = bf16[1,512,1024]{2,1,0:T(8,128)(2,1)} fusion(bf16[512,1024]{1,0:T(8,128)(2,1)} %collective-permute-done.7, bf16[512,512]{0,1:T(8,128)(2,1)S(1)} %bitcast.182, bf16[512,1024]{1,0:T(8,128)(2,1)S(1)} %copy-done), kind=kOutput, calls=%fused_computation.69 | convolution fusion | flops 538443776 | bytes 3670016 | tf_op jit(solution)/shard_map/dot_general | solution.py:151
  (55 shorter events, 0.2 us)
Async XLA Ops:
  0.0 226.5 %copy-start = (bf16[512,1024]{1,0:T(8,128)(2,1)S(1)}, bf16[512,1024]{1,0:T(8,128)(2,1)}, u32[]{:S(2)}) copy-start(bf16[512,1024]{1,0:T(8,128)(2,1)} %param.27) | copy-start | bytes 3145732
  0.0 3.2 %copy-start.2 = (bf16[1,512,1024]{2,1,0:T(8,128)(2,1)S(1)}, bf16[1,512,1024]{2,1,0:T(8,128)(2,1)}, u32[]{:S(2)}) copy-start(bf16[1,512,1024]{2,1,0:T(8,128)(2,1)} %param.22) | copy-start | bytes 3145732
  0.0 3.3 %copy-start.18 = (f32[1024]{0:T(1024)S(1)}, f32[1024]{0:T(1024)}, u32[]{:S(2)}) copy-start(f32[1024]{0:T(1024)} %param.23) | copy-start | bytes 12292
  3.7 25.1 %collective-permute-start = (bf16[512,1024]{1,0:T(8,128)(2,1)S(1)}, bf16[512,1024]{1,0:T(8,128)(2,1)}, u32[]{:S(2)}, u32[]{:S(2)}) collective-permute-start(bf16[512,1024]{1,0:T(8,128)(2,1)S(1)} %fusion.36), channel_id=1, source_target_pairs={{0,1},{1,0},{2,3},{3,2},{4,5},{5,4},{6,7},{7,6},{8,9},{9,8},{10,11... | collective-permute-start | bytes 3145736 | tf_op jit(solution)/shard_map/ppermute | solution.py:18
  15.7 13.0 %copy-start.8 = (bf16[1024,3,512]{0,2,1:T(8,128)(2,1)S(1)}, bf16[1024,3,512]{0,2,1:T(8,128)(2,1)}, u32[]{:S(2)}) copy-start(bf16[1024,3,512]{0,2,1:T(8,128)(2,1)} %copy.20) | copy-start | bytes 9437188
  32.1 1.9 copy-start.1
  32.1 1.9 copy-start.19
  34.5 4.5 %copy-start.20 = (f32[64]{0:T(128)S(1)}, f32[64]{0:T(128)}, u32[]{:S(2)}) copy-start(f32[64]{0:T(128)} %param.25) | copy-start | bytes 772
  34.8 22.7 %collective-permute-start.1 = (bf16[1024,2,8,64]{0,3,2,1:T(8,128)(2,1)S(1)}, bf16[1024,2,8,64]{0,3,2,1:T(8,128)(2,1)S(1)}, u32[]{:S(2)}, u32[]{:S(2)}) collective-permute-start(bf16[1024,2,8,64]{0,3,2,1:T(8,128)(2,1)S(1)} %maximum_maximum_fusion), channel_id=1, source_target_pairs={{0,2},{2,0},{4,6},{6,4},{8,10},{10,8},{12,14},{14,12},{16,18},{18,... | collective-permute-start | bytes 6291464 | tf_op jit(solution)/shard_map/ppermute | solution.py:105
  34.9 48.2 %collective-permute-start.2 = (bf16[1024,2,8,64]{0,3,2,1:T(8,128)(2,1)S(1)}, bf16[1024,2,8,64]{0,3,2,1:T(8,128)(2,1)}, u32[]{:S(2)}, u32[]{:S(2)}) collective-permute-start(bf16[1024,2,8,64]{0,3,2,1:T(8,128)(2,1)S(1)} %maximum_maximum_fusion), channel_id=1, source_target_pairs={{0,4},{2,6},{4,0},{6,2},{8,12},{10,14},{12,8},{14,10},{16,20},{18,... | collective-permute-start | bytes 6291464 | tf_op jit(solution)/shard_map/ppermute | solution.py:105
  36.4 46.6 %collective-permute-start.3 = (bf16[1024,2,8,64]{0,3,2,1:T(8,128)(2,1)S(1)}, bf16[1024,2,8,64]{0,3,2,1:T(8,128)(2,1)S(1)}, u32[]{:S(2)}, u32[]{:S(2)}) collective-permute-start(bf16[1024,2,8,64]{0,3,2,1:T(8,128)(2,1)S(1)} %maximum_maximum_fusion), channel_id=1, source_target_pairs={{2,8},{6,12},{8,2},{10,16},{12,6},{14,20},{16,10},{18,24},{20,14},... | collective-permute-start | bytes 6291464 | tf_op jit(solution)/shard_map/ppermute | solution.py:105
  39.6 9.1 %copy-start.9 = (bf16[512,8,64]{0,2,1:T(8,128)(2,1)}, bf16[512,8,64]{0,2,1:T(8,128)(2,1)S(1)}, u32[]{:S(2)}) copy-start(bf16[512,8,64]{0,2,1:T(8,128)(2,1)S(1)} %get-tuple-element.152) | copy-start | bytes 1572868
  39.6 9.0 %copy-start.11 = (bf16[512,8,64]{0,2,1:T(8,128)(2,1)}, bf16[512,8,64]{0,2,1:T(8,128)(2,1)S(1)}, u32[]{:S(2)}) copy-start(bf16[512,8,64]{0,2,1:T(8,128)(2,1)S(1)} %get-tuple-element.153) | copy-start | bytes 1572868
  57.4 32.7 %copy-start.17 = (s32[16]{0:T(128)S(1)}, s32[16]{0:T(128)}, u32[]{:S(2)}) copy-start(s32[16]{0:T(128)} %param.29) | copy-start | bytes 196
  57.5 26.9 %copy-start.15 = (bf16[1024,2,8,64]{0,3,2,1:T(8,128)(2,1)}, bf16[1024,2,8,64]{0,3,2,1:T(8,128)(2,1)S(1)}, u32[]{:S(2)}) copy-start(bf16[1024,2,8,64]{0,3,2,1:T(8,128)(2,1)S(1)} %collective-permute-done.1) | copy-start | bytes 6291460
  83.0 1.3 copy-start.13
  84.4 79.9 %collective-permute-start.4 = (bf16[1024,2,8,64]{0,3,2,1:T(8,128)(2,1)}, bf16[1024,2,8,64]{0,3,2,1:T(8,128)(2,1)}, u32[]{:S(2)}, u32[]{:S(2)}) collective-permute-start(bf16[1024,2,8,64]{0,3,2,1:T(8,128)(2,1)} %collective-permute-done.2), channel_id=1, source_target_pairs={{0,2},{2,0},{4,6},{6,4},{8,10},{10,8},{12,14},{14,12},{16,18},{18,... | collective-permute-start | bytes 6291464 | tf_op jit(solution)/shard_map/ppermute | solution.py:105
  84.4 79.9 %collective-permute-start.5 = (bf16[1024,2,8,64]{0,3,2,1:T(8,128)(2,1)}, bf16[1024,2,8,64]{0,3,2,1:T(8,128)(2,1)}, u32[]{:S(2)}, u32[]{:S(2)}) collective-permute-start(bf16[1024,2,8,64]{0,3,2,1:T(8,128)(2,1)} %collective-permute-done.2), channel_id=1, source_target_pairs={{0,8},{2,10},{8,16},{10,18},{12,4},{14,6},{16,24},{18,26},{20,12},... | collective-permute-start | bytes 6291464 | tf_op jit(solution)/shard_map/ppermute | solution.py:105
  97.6 10.9 %copy-start.16 = (bf16[1024,2,8,64]{0,3,2,1:T(8,128)(2,1)S(1)}, bf16[1024,2,8,64]{0,3,2,1:T(8,128)(2,1)}, u32[]{:S(2)}) copy-start(bf16[1024,2,8,64]{0,3,2,1:T(8,128)(2,1)} %get-tuple-element.34) | copy-start | bytes 6291460 | tf_op jit(solution)/shard_map/cond
  117.3 1.4 copy-start.3
  138.7 1.3 copy-start.4
  140.0 10.8 %copy-start.14 = (bf16[1024,2,8,64]{0,3,2,1:T(8,128)(2,1)S(1)}, bf16[1024,2,8,64]{0,3,2,1:T(8,128)(2,1)}, u32[]{:S(2)}) copy-start(bf16[1024,2,8,64]{0,3,2,1:T(8,128)(2,1)} %get-tuple-element.38) | copy-start | bytes 6291460 | tf_op jit(solution)/shard_map/cond
  164.3 52.9 %collective-permute-start.6 = (bf16[1024,2,8,64]{0,3,2,1:T(8,128)(2,1)}, bf16[1024,2,8,64]{0,3,2,1:T(8,128)(2,1)}, u32[]{:S(2)}, u32[]{:S(2)}) collective-permute-start(bf16[1024,2,8,64]{0,3,2,1:T(8,128)(2,1)} %collective-permute-done.5), channel_id=1, source_target_pairs={{0,2},{2,0},{4,6},{6,4},{8,10},{10,8},{12,14},{14,12},{16,18},{18,... | collective-permute-start | bytes 6291464 | tf_op jit(solution)/shard_map/ppermute | solution.py:105
  192.2 1.3 copy-start.7
  192.2 21.2 %copy-start.5 = (f32[1024,8,64]{0,2,1:T(8,128)S(1)}, f32[1024,8,64]{0,2,1:T(8,128)}, u32[]{:S(2)}) copy-start(f32[1024,8,64]{0,2,1:T(8,128)} %add_add_fusion.1) | copy-start | bytes 6291460
  213.4 3.7 %copy-start.12 = (bf16[512,8,64]{0,2,1:T(8,128)(2,1)S(1)}, bf16[512,8,64]{0,2,1:T(8,128)(2,1)}, u32[]{:S(2)}) copy-start(bf16[512,8,64]{0,2,1:T(8,128)(2,1)} %copy-done.11) | copy-start | bytes 1572868
  217.1 9.1 %copy-start.6 = (f32[1024,8,64]{0,2,1:T(8,128)S(1)}, f32[1024,8,64]{0,2,1:T(8,128)}, u32[]{:S(2)}) copy-start(f32[1024,8,64]{0,2,1:T(8,128)} %add_add_fusion) | copy-start | bytes 6291460
  226.5 2.2 copy-start.10
  228.2 15.1 %collective-permute-start.7 = (bf16[512,1024]{1,0:T(8,128)(2,1)}, bf16[512,1024]{1,0:T(8,128)(2,1)}, u32[]{:S(2)}, u32[]{:S(2)}) collective-permute-start(bf16[512,1024]{1,0:T(8,128)(2,1)} %convolution_convert_fusion), channel_id=1, source_target_pairs={{0,1},{1,0},{2,3},{3,2},{4,5},{5,4},{6,7},{7,6},{8,9},{9,8},{10,11... | collective-permute-start | bytes 3145736 | tf_op jit(solution)/shard_map/ppermute | solution.py:18
where the time goes:
time: 243 us; the launch traced here: 247 us
  matrix products  147 us (60%)
  waiting for transfers between devices  40.4 us (17%)
  other arithmetic  20.5 us (8%)
  local copies, waits for them, and re-layouts  17 us (7%)
  between operations  12 us (5%)
  starting transfers between devices  8.76 us (4%)
    dot_general x8, matrix products, block_terms(): jnp.einsum('qhd,khd->hqk', queries, key_rows, preferred_element_type=jnp....  72.5 us
    dot_general x8, matrix products, block_terms(): jnp.einsum('hqk,khd->qhd', weights, values, preferred_element_type=jnp.fl...  61.6 us
    ppermute x6, waiting for transfers between devices, routed(): lax.ppermute(block, 'group', [(a, b) for a, b in route if 0 <= b < group_...  25.6 us
    ppermute x2, waiting for transfers between devices, rotated(): return lax.ppermute(block, axis, route)  14.8 us
    unnamed x39, local copies, waits for them, and re-layouts  11.5 us
    dot_general x2, matrix products, project(): projected = jnp.dot(rows, flat_w, preferred_element_type=jnp.float32)  8.58 us
    add x4, other arithmetic, body(): numerator, denominator = (numerator + part_num, denominator + part_den)  8.27 us
    ppermute x6, starting transfers between devices, routed(): lax.ppermute(block, 'group', [(a, b) for a, b in route if 0 <= b < group_...  7.69 us
  transfers between devices with their start and end apart: 8, of which 3 were waited for; matrix products, arithmetic and copies ran while one was open for 63% of the time, Pallas kernels for 0%

commit v1 on v0

v1 whole, which is shorter than its diff:
```python
import functools

import jax
import jax.numpy as jnp
from jax import lax
from jax.sharding import PartitionSpec as P
from jax.experimental import pallas as pl
from jax.experimental.pallas import tpu as pltpu

REACH = 3


def shifted(block, axis, distance):
    devices = range(lax.axis_size(axis))
    route = [(i - distance, i) for i in devices if i - distance in devices]
    return lax.ppermute(block, axis, route)


def rotated(block, axis, distance):
    count = lax.axis_size(axis)
    route = [(i, (i + distance) % count) for i in range(count)]
    return lax.ppermute(block, axis, route)


def norm_rows(values, gain):
    centre = jnp.mean(values, axis=-1, keepdims=True)
    centred = values - centre
    spread = jnp.mean(centred * centred, axis=-1, keepdims=True)
    return centred * lax.rsqrt(spread + 1e-06) * gain


def block_terms(queries, key_rows, values, score_scale):
    scores = (
        jnp.einsum("qhd,khd->hqk", queries, key_rows, preferred_element_type=jnp.float32)
        * score_scale
    )
    weights = jnp.exp(scores).astype(jnp.bfloat16)
    numerator = jnp.einsum("hqk,khd->qhd", weights, values, preferred_element_type=jnp.float32)
    denominator = jnp.transpose(jnp.sum(weights, axis=2, dtype=jnp.float32))
    return (numerator, denominator)


def attention_kernel(q_ref, k_ref, v_ref, num_in, den_in, num_out, den_out, *, head_size, scale):
    queries = q_ref[...]
    keys = k_ref[...]
    values = v_ref[...]
    first = lax.broadcasted_iota(jnp.int32, (1, 2 * head_size), 1) < head_size
    parts = []
    for lanes in (first, jnp.logical_not(first)):
        head_keys = jnp.where(lanes, keys, jnp.zeros_like(keys))
        scores = lax.dot_general(
            queries, head_keys, (((1,), (1,)), ((), ())), preferred_element_type=jnp.float32
        ) * scale
        weights = jnp.exp(scores).astype(jnp.bfloat16)
        numerator = jnp.dot(weights, values, preferred_element_type=jnp.float32)
        denominator = jnp.sum(weights.astype(jnp.float32), axis=1, keepdims=True)
        parts.append((numerator, denominator))
    num_out[...] = num_in[...] + jnp.where(first, parts[0][0], parts[1][0])
    den_out[...] = den_in[...] + jnp.where(first, parts[0][1], parts[1][1])


def attend_block(queries, held, numerator, denominator, row_start, row_count, head_size, scale):
    token_count, width = queries.shape
    key_count = held.shape[1]
    pair_width = 2 * head_size
    tile = min(row_count, 512)
    first_tile = row_start // tile
    row_spec = pl.BlockSpec((tile, pair_width), lambda i, j: (i + first_tile, j))
    key_spec = pl.BlockSpec((None, key_count, pair_width), lambda i, j: (0, 0, j))
    value_spec = pl.BlockSpec((None, key_count, pair_width), lambda i, j: (1, 0, j))
    flops = 2 * 2 * 2 * row_count * key_count * width
    return pl.pallas_call(
        functools.partial(attention_kernel, head_size=head_size, scale=scale),
        grid=(row_count // tile, width // pair_width),
        in_specs=[row_spec, key_spec, value_spec, row_spec, row_spec],
        out_specs=[row_spec, row_spec],
        out_shape=[jax.ShapeDtypeStruct((token_count, width), jnp.float32)] * 2,
        input_output_aliases={3: 0, 4: 1},
        compiler_params=pltpu.CompilerParams(dimension_semantics=("arbitrary", "arbitrary")),
        cost_estimate=pl.CostEstimate(
            flops=flops,
            transcendentals=row_count * key_count * (width // head_size),
            bytes_accessed=row_count * width * 18 + key_count * width * 4 * (row_count // tile),
        ),
    )(queries, held, held, numerator, denominator)


def body(tokens, norm_gain, w_qkv, q_gain, k_gain, w_out, covis_mask, capture_rank):
    full_width = tokens.shape[2]
    local_width = w_qkv.shape[2]
    head_size = q_gain.shape[0]
    heads_here = local_width // head_size
    score_scale = head_size ** (-0.5)
    slab_count = lax.axis_size("slab")
    my_group = lax.axis_index("group")
    group_count = lax.axis_size("group")
    normed = norm_rows(tokens[0].astype(jnp.float32), norm_gain).astype(jnp.bfloat16)
    piece_rows = normed.shape[0]
    flat_w = w_qkv.reshape(full_width, 3 * local_width)

    def project(rows):
        projected = jnp.dot(rows, flat_w, preferred_element_type=jnp.float32)
        projected = projected.reshape(rows.shape[0], 3, heads_here, head_size)
        queries = norm_rows(projected[:, 0], q_gain).astype(jnp.bfloat16)
        key_rows = norm_rows(projected[:, 1], k_gain).astype(jnp.bfloat16)
        values = projected[:, 2].astype(jnp.bfloat16)
        flat = (rows.shape[0], local_width)
        return queries.reshape(flat), jnp.stack([key_rows.reshape(flat), values.reshape(flat)])

    queries, pairs = project(normed)
    if slab_count > 1:
        others = jnp.concatenate(
            [rotated(normed, "slab", k) for k in range(1, slab_count)], axis=0
        )
        rest_q, rest_pairs = project(others)
        queries = jnp.concatenate([queries, rest_q], axis=0)
        pairs = jnp.concatenate([pairs, rest_pairs], axis=1)
    token_count = queries.shape[0]

    def allowed_from(source):
        in_range = (source >= 0) & (source < group_count)
        clipped = jnp.clip(source, 0, group_count - 1)
        return (
            in_range
            & (covis_mask[my_group, clipped] == 1)
            & (capture_rank[clipped] <= capture_rank[my_group])
        )

    def add_terms(held, sums, row_start=0, row_count=None):
        row_count = token_count if row_count is None else row_count
        return tuple(
            attend_block(queries, held, sums[0], sums[1], row_start, row_count, head_size, score_scale)
        )

    def add_masked(source, held, sums, row_start=0, row_count=None):
        return lax.cond(
            allowed_from(source),
            lambda: add_terms(held, sums, row_start, row_count),
            lambda: sums,
        )

    def routed(block, route):
        return lax.ppermute(block, "group", [(a, b) for a, b in route if 0 <= b < group_count])

    g_all = range(group_count)
    spot = my_group % 4
    low = spot < 2
    even = spot % 2 == 0
    on_chip = [(g, g ^ 1) for g in g_all]
    across_x = [(g, g ^ 2) for g in g_all]
    along_z_once = [(g, g + 3) if g % 2 == 1 else (g, g - 3) for g in g_all]
    along_z_relay = [(g, g + 4) if g % 4 < 2 else (g, g - 4) for g in g_all]

    round_one = [
        (my_group ^ 1, routed(pairs, on_chip)),
        (my_group ^ 2, routed(pairs, across_x)),
        (jnp.where(even, my_group - 3, my_group + 3), routed(pairs, along_z_once)),
    ]
    zeros = jnp.zeros((token_count, local_width), jnp.float32)
    sums = add_terms(pairs, (zeros, zeros))
    round_one, sums = lax.optimization_barrier((round_one, sums))
    from_x = round_one[1][1]
    round_two = [
        (my_group ^ 3, routed(from_x, on_chip)),
        (jnp.where(low, my_group - 2, my_group + 2), routed(from_x, along_z_relay)),
    ]
    for source, held in round_one:
        sums = add_masked(source, held, sums)
    round_two, sums = lax.optimization_barrier((round_two, sums))
    from_z = round_two[1][1]
    last_source = jnp.where(
        spot == 0, my_group - 1, jnp.where(spot == 1, my_group - 3, jnp.where(spot == 2, my_group + 3, my_group + 1))
    )
    last_held = routed(from_z, on_chip)
    for source, held in round_two:
        sums = add_masked(source, held, sums)
    last_held, sums = lax.optimization_barrier((last_held, sums))

    mixed = None
    for k in list(range(1, slab_count)) + [0]:
        row_start = k * piece_rows
        sums = add_masked(last_source, last_held, sums, row_start, piece_rows)
        rows = slice(row_start, row_start + piece_rows)
        attended = (sums[0][rows] / sums[1][rows]).astype(jnp.bfloat16)
        chunk = jnp.dot(attended, w_out, preferred_element_type=jnp.float32)
        if k != 0:
            outgoing, last_held, sums = lax.optimization_barrier(
                (chunk.astype(jnp.bfloat16), last_held, sums)
            )
            chunk = rotated(outgoing, "slab", -k).astype(jnp.float32)
        mixed = chunk if mixed is None else mixed + chunk
    return mixed.astype(jnp.bfloat16)[None]


def solution(mesh):
    placed = (
        P("group", "slab", None),
        P(),
        P(None, None, "slab"),
        P(),
        P(),
        P("slab", None),
        P(),
        P(),
    )
    return jax.shard_map(
        body, mesh=mesh, in_specs=placed, out_specs=P("group", "slab", None), check_vma=False
    )
```

time: 243 us -> 204 us (0.84)
  the two profiles are of different devices: /device:TPU:20 before, /device:TPU:9 now
where the time goes in v1:
time: 204 us; the launch traced here: 203 us
  Pallas kernels  56.1 us (28%)
  waiting for transfers between devices  54.1 us (27%)
  local copies, waits for them, and re-layouts  35.2 us (17%)
  other arithmetic  17.3 us (8%)
  matrix products  14.8 us (7%)
  starting transfers between devices  13.5 us (7%)
  between operations  11.6 us (6%)
    pallas_call x5, Pallas kernels, attend_block(): pl.pallas_call(functools.partial(attention_kernel, head_size=head_size, s...  56.1 us
    ppermute x6, waiting for transfers between devices, routed(): lax.ppermute(block, 'group', [(a, b) for a, b in route if 0 <= b < group_...  39.5 us
    ppermute x2, waiting for transfers between devices, rotated(): return lax.ppermute(block, axis, route)  14.6 us
    ppermute x6, starting transfers between devices, routed(): lax.ppermute(block, 'group', [(a, b) for a, b in route if 0 <= b < group_...  11.1 us
    dot_general x2, matrix products, project(): projected = jnp.dot(rows, flat_w, preferred_element_type=jnp.float32)  7.94 us
    dot_general x2, matrix products, body(): chunk = jnp.dot(attended, w_out, preferred_element_type=jnp.float32)  6.88 us
    mul x12, local copies, waits for them, and re-layouts, norm_rows(): return centred * lax.rsqrt(spread + 1e-06) * gain  5.93 us
    sub x8, local copies, waits for them, and re-layouts, norm_rows(): centred = values - centre  5.78 us
  transfers between devices with their start and end apart: 8, of which 4 were waited for; matrix products, arithmetic and copies ran while one was open for 18% of the time, Pallas kernels for 24%

profile of v1, /device:TPU:9, one launch (start us, length us, event | category | flops | bytes accessed | tf_op | source)
XLA Modules:
  0.0 202.7 jit_solution(16372364244841650633)
XLA Ops:
  0.0 1.6 convert_reduce_fusion
  1.6 1.6 fusion.6
  3.3 1.4 fusion.8
  4.6 1.2 collective-permute-start
  5.9 4.6 %copy.39 = bf16[1024,3,512]{0,2,1:T(8,128)(2,1)} copy(bf16[1024,3,512]{2,0,1:T(8,128)(2,1)} %param.24) | data formatting | bytes 6291456 | tf_op args[2]
  10.5 3.9 %fusion.11 = f32[512,3,8,64]{0,3,2,1:T(8,128)S(1)} fusion(bf16[3,8,64,1024]{3,2,1,0:T(8,128)(2,1)} %bitcast.99, bf16[1,512,1024]{2,1,0:T(8,128)(2,1)S(1)} %copy-done.2, f32[1024]{0:T(1024)S(1)} %copy-done.10, f32[512]{0:T(512)S(1)} %add_rsqrt_fusion.4, f32[512]{0:T(512)S(1)} %broadcast_multiply_fusion.4), kind=kOutput, calls=%fused_computation.17 | convolution fusion | flops 1613234176 | bytes 7348224 | tf_op jit(solution)/shard_map/dot_general | solution.py:102
  14.4 0.9 slice.90
  15.3 1.2 slice_reduce_fusion.1
  16.6 0.3 fusion.20
  16.9 0.1 mul.155
  17.0 1.3 copy.42
  18.3 0.1 sub.93
  18.5 1.3 copy.41
  19.8 2.6 %copy.40 = f32[1,512,512]{2,1,0:T(8,128)} copy(f32[1,512,512]{1,2,0:T(8,128)} %bitcast.98) | data formatting | bytes 2097152 | tf_op jit(solution)/shard_map/squeeze | solution.py:105
  22.5 1.1 copy.43
  23.5 5.4 %collective-permute-done = bf16[512,1024]{1,0:T(8,128)(2,1)} collective-permute-done((bf16[512,1024]{1,0:T(8,128)(2,1)}, bf16[512,1024]{1,0:T(8,128)(2,1)}, u32[]{:S(2)}, u32[]{:S(2)}) %collective-permute-start) | collective-permute-done | bytes 1048608 | tf_op jit(solution)/shard_map/ppermute | solution.py:22
  29.0 4.1 %fusion.13 = f32[512,3,8,64]{0,3,2,1:T(8,128)S(1)} fusion(bf16[3,8,64,1024]{3,2,1,0:T(8,128)(2,1)} %bitcast.100, bf16[512,1024]{1,0:T(8,128)(2,1)} %collective-permute-done), kind=kOutput, calls=%fused_computation.21 | convolution fusion | flops 1610612736 | bytes 7340032 | tf_op jit(solution)/shard_map/dot_general | solution.py:102
  33.0 1.6 slice_reduce_fusion
  34.6 0.9 slice.89
  35.5 0.3 fusion.18
  35.8 0.1 mul.167
  36.0 1.3 copy.46
  37.4 1.3 copy.45
  38.7 2.6 %copy.44 = f32[1,512,512]{2,1,0:T(8,128)} copy(f32[1,512,512]{1,2,0:T(8,128)} %bitcast.97) | data formatting | bytes 2097152 | tf_op jit(solution)/shard_map/squeeze | solution.py:105
  41.4 2.0 %copy.47 = bf16[1,512,512]{2,1,0:T(8,128)(2,1)} copy(bf16[1,512,512]{1,2,0:T(8,128)(2,1)} %bitcast.102) | data formatting | bytes 1048576 | tf_op jit(solution)/shard_map/convert_element_type | solution.py:106
  43.4 3.4 %multiply_convert_fusion.3 = (bf16[1,512,512]{2,1,0:T(8,128)(2,1)S(1)}, bf16[1,512,512]{2,1,0:T(8,128)(2,1)S(1)}) fusion(f32[1,512,512]{2,1,0:T(8,128)S(1)} %copy-done.4, f32[1,512,512]{2,1,0:T(8,128)} %copy.40, f32[1,512,512]{2,1,0:T(8,128)} %copy.41, f32[512]{0:T(512)S(1)} %mul.159, f32[1,512,512]{2,1,0:T(8,128)} %copy.46, f32[1,512,512]{2,1,0:T(8,128)} %copy.44, ...), kind=kLoop, calls=%fused_computation.42 | loop fusion | flops 2097152 | bytes 7342080 | tf_op jit(solution)/shard_map/convert_element_type | solution.py:105
  46.8 1.5 maximum_maximum_fusion.k_ref.v_ref
  48.3 1.5 collective-permute-start.1
  49.9 1.2 collective-permute-start.2
  51.1 3.5 %collective-permute-start.3 = (bf16[2,1024,512]{2,1,0:T(8,128)(2,1)}, bf16[2,1024,512]{2,1,0:T(8,128)(2,1)}, u32[]{:S(2)}, u32[]{:S(2)}) collective-permute-start(bf16[2,1024,512]{2,1,0:T(8,128)(2,1)} %maximum_maximum_fusion.k_ref.v_ref), channel_id=1, source_target_pairs={{2,8},{6,12},{8,2},{10,16},{12,6},{14,20},{16,10},{18,24},{20,14},... | collective-permute-start | bytes 6291464 | tf_op jit(solution)/shard_map/ppermute | solution.py:143
  54.7 0.1 mul.172
  54.8 1.3 copy.50
  56.2 1.3 copy.49
  57.5 1.3 copy.48
  58.9 0.1 mul.180
  59.1 1.3 copy.53
  60.5 1.4 copy.52
  61.9 1.3 copy.51
  63.2 3.3 %multiply_convert_fusion.1 = (bf16[512,512]{1,0:T(8,128)(2,1)S(1)}, bf16[512,512]{1,0:T(8,128)(2,1)S(1)}) fusion(f32[512,512]{1,0:T(8,128)S(1)} %copy-done.5, f32[512,512]{1,0:T(8,128)} %copy.48, f32[512,512]{1,0:T(8,128)} %copy.49, f32[512]{0:T(512)S(1)} %mul.176, f32[512,512]{1,0:T(8,128)} %copy.53, f32[512,512]{1,0:T(8,128)} %copy.51, f32[512,512]{1,0:T(8,128)} %copy.52), kind=kLoop, calls=%fused_computation.40 | loop fusion | flops 2097152 | bytes 7342080 | tf_op jit(solution)/shard_map/convert_element_type | solution.py:104
  66.5 1.0 pad_maximum_fusion.q_ref
  67.6 0.2 broadcast_in_dim.4.num_in
  67.8 1.6 broadcast_in_dim.4.clone.den_in
  69.4 13.6 %shard_map.82 = (f32[1024,512]{1,0:T(8,128)S(1)}, f32[1024,512]{1,0:T(8,128)}) custom-call(bf16[1024,512]{1,0:T(8,128)(2,1)} %pad_maximum_fusion.q_ref, bf16[2,1024,512]{2,1,0:T(8,128)(2,1)} %maximum_maximum_fusion.k_ref.v_ref, bf16[2,1024,512]{2,1,0:T(8,128)(2,1)} %maximum_maximum_fusion.k_ref.v_ref, ...), custom_call_target="tpu_custom_call", output_to_operand_aliasing={{0}: (3, {}), {1}: (4, {})} | custom-call | flops 4294967296 | bytes 13631488 | tf_op jit(solution)/shard_map/pallas_call | solution.py:72
  83.0 14.4 %collective-permute-done.2 = bf16[2,1024,512]{2,1,0:T(8,128)(2,1)} collective-permute-done((bf16[2,1024,512]{2,1,0:T(8,128)(2,1)}, bf16[2,1024,512]{2,1,0:T(8,128)(2,1)}, u32[]{:S(2)}, u32[]{:S(2)}) %collective-permute-start.2) | collective-permute-done | bytes 2097184 | tf_op jit(solution)/shard_map/ppermute | solution.py:143
  97.4 0.8 collective-permute-start.4
  98.2 3.2 %collective-permute-start.5 = (bf16[2,1024,512]{2,1,0:T(8,128)(2,1)}, bf16[2,1024,512]{2,1,0:T(8,128)(2,1)}, u32[]{:S(2)}, u32[]{:S(2)}) collective-permute-start(bf16[2,1024,512]{2,1,0:T(8,128)(2,1)} %collective-permute-done.2), channel_id=1, source_target_pairs={{0,8},{2,10},{8,16},{10,18},{12,4},{14,6},{16,24},{18,26},{20,12},... | collective-permute-start | bytes 6291464 | tf_op jit(solution)/shard_map/ppermute | solution.py:143
  101.5 0.6 fusion.36
  103.3 1.4 fusion.34
  108.9 13.6 %conditional.8 = ((f32[1024,512]{1,0:T(8,128)S(1)}, f32[1024,512]{1,0:T(8,128)})) conditional(s32[]{:T(128)} %convert_element_type.112, (f32[1024,512]{1,0:T(8,128)S(1)}, f32[1024,512]{1,0:T(8,128)}) %get-tuple-element.318, (bf16[1024,512]{1,0:T(8,128)(2,1)}, bf16[2,1024,512]{2,1,0:T(8,128)(2,1)}, f32[1024,512]{1,0:T(8,128)S(1)}, ...), branch_computations={%region_12.13_spmd, %region_13.14_spmd} | conditional | flops 4294967296 | bytes 13631496 | solution.py:136
  109.0 13.6 %branch_1_fun.10 = (f32[1024,512]{1,0:T(8,128)S(1)}, f32[1024,512]{1,0:T(8,128)}) custom-call(bf16[1024,512]{1,0:T(8,128)(2,1)} %get-tuple-element.132.q_ref, bf16[2,1024,512]{2,1,0:T(8,128)(2,1)} %get-tuple-element.133.k_ref.v_ref, bf16[2,1024,512]{2,1,0:T(8,128)(2,1)} %get-tuple-element.133.k_ref.v_ref, ...), custom_call_target="tpu_custom_call", output_to_operand_aliasing={{0}: (3, {}), {1}: (4, {})} | custom-call | flops 4294967296 | bytes 13631488 | tf_op jit(solution)/shard_map/cond/branch_1_fun/pallas_call | solution.py:72
  122.6 25.1 %collective-permute-done.5 = bf16[2,1024,512]{2,1,0:T(8,128)(2,1)} collective-permute-done((bf16[2,1024,512]{2,1,0:T(8,128)(2,1)}, bf16[2,1024,512]{2,1,0:T(8,128)(2,1)}, u32[]{:S(2)}, u32[]{:S(2)}) %collective-permute-start.5) | collective-permute-done | bytes 2097184 | tf_op jit(solution)/shard_map/ppermute | solution.py:143
  147.7 0.8 collective-permute-start.6
  148.5 0.7 fusion.35
  150.4 1.5 fusion.33
  156.4 13.4 %conditional.10 = ((f32[1024,512]{1,0:T(8,128)}, f32[1024,512]{1,0:T(8,128)})) conditional(s32[]{:T(128)} %convert_element_type.115, (f32[1024,512]{1,0:T(8,128)}, f32[1024,512]{1,0:T(8,128)}) %tuple.152, (bf16[1024,512]{1,0:T(8,128)(2,1)}, bf16[2,1024,512]{2,1,0:T(8,128)(2,1)}, f32[1024,512]{1,0:T(8,128)}, f32[1024,512]{1,0:T(8,128)}) %tuple.151), branch_computations={%region_16.17_spmd, %region_17.18_spmd} | conditional | flops 4294967296 | bytes 13631496 | solution.py:136
  156.5 13.4 %branch_1_fun.12 = (f32[1024,512]{1,0:T(8,128)}, f32[1024,512]{1,0:T(8,128)}) custom-call(bf16[1024,512]{1,0:T(8,128)(2,1)} %get-tuple-element.140.q_ref, bf16[2,1024,512]{2,1,0:T(8,128)(2,1)} %get-tuple-element.141.k_ref.v_ref, bf16[2,1024,512]{2,1,0:T(8,128)(2,1)} %get-tuple-element.141.k_ref.v_ref, ...), custom_call_target="tpu_custom_call", output_to_operand_aliasing={{0}: (3, {}), {1}: (4, {})} | custom-call | flops 4294967296 | bytes 13631488 | tf_op jit(solution)/shard_map/cond/branch_1_fun/pallas_call | solution.py:72
  169.9 7.8 %conditional.12 = ((f32[1024,512]{1,0:T(8,128)}, f32[1024,512]{1,0:T(8,128)})) conditional(s32[]{:T(128)} %convert_element_type.99, (f32[1024,512]{1,0:T(8,128)}, f32[1024,512]{1,0:T(8,128)}) %get-tuple-element.322, (bf16[1024,512]{1,0:T(8,128)(2,1)}, bf16[2,1024,512]{2,1,0:T(8,128)(2,1)S(1)}, f32[1024,512]{1,0:T(8,128)}, ...), branch_computations={%region_20.21_spmd.clone, %region_21.22_spmd.clone} | conditional | flops 2147483648 | bytes 6815752 | solution.py:136
  169.9 7.7 %branch_1_fun.15 = (f32[1024,512]{1,0:T(8,128)}, f32[1024,512]{1,0:T(8,128)}) custom-call(bf16[1024,512]{1,0:T(8,128)(2,1)} %get-tuple-element.249.q_ref, bf16[2,1024,512]{2,1,0:T(8,128)(2,1)S(1)} %get-tuple-element.250.k_ref.v_ref, bf16[2,1024,512]{2,1,0:T(8,128)(2,1)S(1)} %get-tuple-element.250.k_ref.v_ref, ...), custom_call_target="tpu_custom_call", output_to_operand_aliasing={{0}: (3, {}), {1}: (4, {})} | custom-call | flops 2147483648 | bytes 6815744 | tf_op jit(solution)/shard_map/cond/branch_1_fun/pallas_call | solution.py:72
  177.6 3.3 %convolution_convert_fusion = bf16[512,1024]{1,0:T(8,128)(2,1)} fusion(bf16[512,1024]{1,0:T(8,128)(2,1)S(1)} %copy-done, f32[1024,512]{1,0:T(8,128)} %get-tuple-element.228, f32[1024,512]{1,0:T(8,128)} %get-tuple-element.227), kind=kOutput, calls=%fused_computation.14 | convolution fusion | flops 537919488 | bytes 4194304 | tf_op jit(solution)/shard_map/dot_general | solution.py:185
  181.0 1.2 collective-permute-start.7
  182.2 7.8 %conditional.13 = ((f32[1024,512]{1,0:T(8,128)}, f32[1024,512]{1,0:T(8,128)})) conditional(s32[]{:T(128)} %convert_element_type.99, (f32[1024,512]{1,0:T(8,128)}, f32[1024,512]{1,0:T(8,128)}) %tuple.85, (bf16[1024,512]{1,0:T(8,128)(2,1)}, bf16[2,1024,512]{2,1,0:T(8,128)(2,1)S(1)}, f32[1024,512]{1,0:T(8,128)}, f32[1024,512]{1,0:T(8,128)}) %tuple.86), branch_computations={%region_22.23_spmd, %region_23.24_spmd} | conditional | flops 2147483648 | bytes 6815768 | solution.py:136
  182.2 7.8 %branch_1_fun.14 = (f32[1024,512]{1,0:T(8,128)}, f32[1024,512]{1,0:T(8,128)}) custom-call(bf16[1024,512]{1,0:T(8,128)(2,1)} %get-tuple-element.152.q_ref, bf16[2,1024,512]{2,1,0:T(8,128)(2,1)S(1)} %get-tuple-element.153.k_ref.v_ref, bf16[2,1024,512]{2,1,0:T(8,128)(2,1)S(1)} %get-tuple-element.153.k_ref.v_ref, ...), custom_call_target="tpu_custom_call", output_to_operand_aliasing={{0}: (3, {}), {1}: (4, {})} | custom-call | flops 2147483648 | bytes 6815744 | tf_op jit(solution)/shard_map/cond/branch_1_fun/pallas_call | solution.py:72
  190.0 9.2 %collective-permute-done.7 = bf16[512,1024]{1,0:T(8,128)(2,1)} collective-permute-done((bf16[512,1024]{1,0:T(8,128)(2,1)}, bf16[512,1024]{1,0:T(8,128)(2,1)}, u32[]{:S(2)}, u32[]{:S(2)}) %collective-permute-start.7) | collective-permute-done | bytes 1048608 | tf_op jit(solution)/shard_map/ppermute | solution.py:22
  199.1 3.5 %fusion.9 = bf16[1,512,1024]{2,1,0:T(8,128)(2,1)} fusion(bf16[512,1024]{1,0:T(8,128)(2,1)} %collective-permute-done.7, bf16[512,1024]{1,0:T(8,128)(2,1)S(1)} %copy-done, f32[1024,512]{1,0:T(8,128)} %get-tuple-element.244, f32[1024,512]{1,0:T(8,128)} %get-tuple-element.243), kind=kOutput, calls=%fused_computation.15 | convolution fusion | flops 538968064 | bytes 5242880 | tf_op jit(solution)/shard_map/dot_general | solution.py:185
  (48 shorter events, 0.6 us)
Async XLA Ops:
  0.0 177.6 %copy-start = (bf16[512,1024]{1,0:T(8,128)(2,1)S(1)}, bf16[512,1024]{1,0:T(8,128)(2,1)}, u32[]{:S(2)}) copy-start(bf16[512,1024]{1,0:T(8,128)(2,1)} %param.27) | copy-start | bytes 3145732
  0.0 3.2 %copy-start.2 = (bf16[1,512,1024]{2,1,0:T(8,128)(2,1)S(1)}, bf16[1,512,1024]{2,1,0:T(8,128)(2,1)}, u32[]{:S(2)}) copy-start(bf16[1,512,1024]{2,1,0:T(8,128)(2,1)} %param.22) | copy-start | bytes 3145732
  0.0 3.3 %copy-start.10 = (f32[1024]{0:T(1024)S(1)}, f32[1024]{0:T(1024)}, u32[]{:S(2)}) copy-start(f32[1024]{0:T(1024)} %param.23) | copy-start | bytes 12292
  4.6 24.3 %collective-permute-start = (bf16[512,1024]{1,0:T(8,128)(2,1)}, bf16[512,1024]{1,0:T(8,128)(2,1)}, u32[]{:S(2)}, u32[]{:S(2)}) collective-permute-start(bf16[512,1024]{1,0:T(8,128)(2,1)} %fusion.8), channel_id=1, source_target_pairs={{0,1},{1,0},{2,3},{3,2},{4,5},{5,4},{6,7},{7,6},{8,9},{9,8},{10,11... | collective-permute-start | bytes 3145736 | tf_op jit(solution)/shard_map/ppermute | solution.py:22
  18.5 3.9 %copy-start.11 = (f32[64]{0:T(128)S(1)}, f32[64]{0:T(128)}, u32[]{:S(2)}) copy-start(f32[64]{0:T(128)} %param.26) | copy-start | bytes 772
  19.8 2.7 %copy-start.6 = (bf16[512,1,8,64]{0,3,2,1:T(8,128)(2,1)S(1)}, bf16[512,1,8,64]{0,3,2,1:T(8,128)(2,1)}, u32[]{:S(2)}) copy-start(bf16[512,1,8,64]{0,3,2,1:T(8,128)(2,1)} %slice.90) | copy-start | bytes 1572868
  38.7 4.7 %copy-start.4 = (f32[1,512,512]{2,1,0:T(8,128)S(1)}, f32[1,512,512]{2,1,0:T(8,128)}, u32[]{:S(2)}) copy-start(f32[1,512,512]{2,1,0:T(8,128)} %copy.42) | copy-start | bytes 3145732
  43.4 3.4 %copy-start.7 = (bf16[1,512,512]{2,1,0:T(8,128)(2,1)S(1)}, bf16[1,512,512]{2,1,0:T(8,128)(2,1)}, u32[]{:S(2)}) copy-start(bf16[1,512,512]{2,1,0:T(8,128)(2,1)} %copy.43) | copy-start | bytes 1572868
  43.4 3.4 %copy-start.8 = (bf16[1,512,512]{2,1,0:T(8,128)(2,1)S(1)}, bf16[1,512,512]{2,1,0:T(8,128)(2,1)}, u32[]{:S(2)}) copy-start(bf16[1,512,512]{2,1,0:T(8,128)(2,1)} %copy.47) | copy-start | bytes 1572868
  48.3 34.7 %collective-permute-start.1 = (bf16[2,1024,512]{2,1,0:T(8,128)(2,1)}, bf16[2,1024,512]{2,1,0:T(8,128)(2,1)}, u32[]{:S(2)}, u32[]{:S(2)}) collective-permute-start(bf16[2,1024,512]{2,1,0:T(8,128)(2,1)} %maximum_maximum_fusion.k_ref.v_ref), channel_id=1, source_target_pairs={{0,2},{2,0},{4,6},{6,4},{8,10},{10,8},{12,14},{14,12},{16,18},{18,... | collective-permute-start | bytes 6291464 | tf_op jit(solution)/shard_map/ppermute | solution.py:143
  49.9 47.6 %collective-permute-start.2 = (bf16[2,1024,512]{2,1,0:T(8,128)(2,1)}, bf16[2,1024,512]{2,1,0:T(8,128)(2,1)}, u32[]{:S(2)}, u32[]{:S(2)}) collective-permute-start(bf16[2,1024,512]{2,1,0:T(8,128)(2,1)} %maximum_maximum_fusion.k_ref.v_ref), channel_id=1, source_target_pairs={{0,4},{2,6},{4,0},{6,2},{8,12},{10,14},{12,8},{14,10},{16,20},{18,... | collective-permute-start | bytes 6291464 | tf_op jit(solution)/shard_map/ppermute | solution.py:143
  51.1 46.4 %collective-permute-start.3 = (bf16[2,1024,512]{2,1,0:T(8,128)(2,1)}, bf16[2,1024,512]{2,1,0:T(8,128)(2,1)}, u32[]{:S(2)}, u32[]{:S(2)}) collective-permute-start(bf16[2,1024,512]{2,1,0:T(8,128)(2,1)} %maximum_maximum_fusion.k_ref.v_ref), channel_id=1, source_target_pairs={{2,8},{6,12},{8,2},{10,16},{12,6},{14,20},{16,10},{18,24},{20,14},... | collective-permute-start | bytes 6291464 | tf_op jit(solution)/shard_map/ppermute | solution.py:143
  56.2 2.6 %copy-start.12 = (f32[64]{0:T(128)S(1)}, f32[64]{0:T(128)}, u32[]{:S(2)}) copy-start(f32[64]{0:T(128)} %param.25) | copy-start | bytes 772
  60.4 1.5 copy-start.3
  61.9 1.3 copy-start.5
  69.4 32.0 %copy-start.9 = (s32[16]{0:T(128)S(1)}, s32[16]{0:T(128)}, u32[]{:S(2)}) copy-start(s32[16]{0:T(128)} %param.29) | copy-start | bytes 196
  97.4 25.1 %collective-permute-start.4 = (bf16[2,1024,512]{2,1,0:T(8,128)(2,1)}, bf16[2,1024,512]{2,1,0:T(8,128)(2,1)}, u32[]{:S(2)}, u32[]{:S(2)}) collective-permute-start(bf16[2,1024,512]{2,1,0:T(8,128)(2,1)} %collective-permute-done.2), channel_id=1, source_target_pairs={{0,2},{2,0},{4,6},{6,4},{8,10},{10,8},{12,14},{14,12},{16,18},{18,... | collective-permute-start | bytes 6291464 | tf_op jit(solution)/shard_map/ppermute | solution.py:143
  98.2 49.5 %collective-permute-start.5 = (bf16[2,1024,512]{2,1,0:T(8,128)(2,1)}, bf16[2,1024,512]{2,1,0:T(8,128)(2,1)}, u32[]{:S(2)}, u32[]{:S(2)}) collective-permute-start(bf16[2,1024,512]{2,1,0:T(8,128)(2,1)} %collective-permute-done.2), channel_id=1, source_target_pairs={{0,8},{2,10},{8,16},{10,18},{12,4},{14,6},{16,24},{18,26},{20,12},... | collective-permute-start | bytes 6291464 | tf_op jit(solution)/shard_map/ppermute | solution.py:143
  122.6 25.1 %copy-start.1 = (f32[1024,512]{1,0:T(8,128)}, f32[1024,512]{1,0:T(8,128)S(1)}, u32[]{:S(2)}) copy-start(f32[1024,512]{1,0:T(8,128)S(1)} %get-tuple-element.214) | copy-start | bytes 6291460
  147.7 22.2 %collective-permute-start.6 = (bf16[2,1024,512]{2,1,0:T(8,128)(2,1)}, bf16[2,1024,512]{2,1,0:T(8,128)(2,1)S(1)}, u32[]{:S(2)}, u32[]{:S(2)}) collective-permute-start(bf16[2,1024,512]{2,1,0:T(8,128)(2,1)} %collective-permute-done.5), channel_id=1, source_target_pairs={{0,2},{2,0},{4,6},{6,4},{8,10},{10,8},{12,14},{14,12},{16,18},{18,... | collective-permute-start | bytes 6291464 | tf_op jit(solution)/shard_map/ppermute | solution.py:143
  181.0 18.2 %collective-permute-start.7 = (bf16[512,1024]{1,0:T(8,128)(2,1)}, bf16[512,1024]{1,0:T(8,128)(2,1)}, u32[]{:S(2)}, u32[]{:S(2)}) collective-permute-start(bf16[512,1024]{1,0:T(8,128)(2,1)} %convolution_convert_fusion), channel_id=1, source_target_pairs={{0,1},{1,0},{2,3},{3,2},{4,5},{5,4},{6,7},{7,6},{8,9},{9,8},{10,11... | collective-permute-start | bytes 3145736 | tf_op jit(solution)/shard_map/ppermute | solution.py:22
